TPU v7x, 32 devices: a whole 2x2x4 slice. The times are simulated.
32 devices in a mesh: ri: 4 (over z), ao: 8 (over y, x, core).
Axes of the slice: x: 2, y: 2, z: 4, core: 2. Of those that a mesh axis runs over, the one named last changes fastest.
Arguments:
- tensor: bfloat16 [512, 256, 256], P('ri', 'ao'), may hold values from -0.5 to 0.5
- live_blocks: int32 [8, 8, 8], P('ri', 'ao'), may hold values 0 or 1
- occ_density: bfloat16 [256, 256], P('ao'), may hold values from -0.375 to 0.375
- virt_density: bfloat16 [256, 256], P('ao'), may hold values from -0.375 to 0.375
- occ_mask: int32 [8, 8], P('ao'), may hold values 0 or 1
- virt_mask: int32 [8, 8], P('ao'), may hold values 0 or 1
- pair_slots: int32 [8, 8], P('ao'), may hold values from 0 to 7, as said below
Outputs:
- polar: float32 [512, 512], P('ri', 'ao')
Inputs may be any that keep to these rules, and one draw needn't show every extreme that they name: pair_slots[b, 0] = b, and the 8 entries of a row are different AO blocks.
All inputs are finite; a program needn't handle non-finite values. No bound on the sum of `live_blocks` or of `occ_mask` or of `virt_mask` on one device may be relied on, other than what follows from the above.
Results may differ from a plain program's by a relative error of at most 0.0041.
Values may be sent and summed in bfloat16 or wider, within the bound.
No kernel may reach another device: no remote copies, remote signals or barrier semaphores. Data moves between devices by JAX's collectives and lax.ppermute only.
A program may use at most 192 MiB of HBM per device.

v0:
```python
import jax
import jax.numpy as jnp
from jax import lax
from jax.experimental.layout import Layout, with_layout_constraint
from jax.sharding import PartitionSpec as P

BS = 32
KS = 8
RB = 64


def screen_density(density, block_mask):
    own_blocks = block_mask.shape[0]
    all_blocks = block_mask.shape[1]
    shaped = density.reshape(own_blocks, BS, all_blocks, BS)
    keeper = block_mask.astype(density.dtype)[:, None, :, None]
    return (shaped * keeper).reshape(density.shape)


def pair_routes(size):
    routes = []
    for dist in range(1, size // 2 + 1):
        if 2 * dist < size:
            route = [(r, (r + dist) % size) for r in range(size)]
        else:
            route = []
            for i in range(size // 2):
                if i % 2 == 0:
                    route.append((i, i + dist))
                else:
                    route.append((i + dist, i))
        recv_from = list(range(size))
        send_to = list(range(size))
        for src, dst in route:
            recv_from[dst] = src
            send_to[src] = dst
        routes.append((route, recv_from, send_to))
    return routes


def mask_slab(slab, live):
    keeper = jnp.repeat(jnp.repeat(live[:, 0, :].astype(slab.dtype), RB, axis=0), BS, axis=1)
    return slab * keeper[:, None, :]


def split_hi_lo(values):
    rounded = lax.reduce_precision(values, exponent_bits=8, mantissa_bits=7)
    return (rounded.astype(jnp.bfloat16), (values - rounded).astype(jnp.bfloat16))


def weight_pair(values):
    hi, lo = split_hi_lo(values)
    both = jnp.stack([hi, lo])
    return both.transpose(2, 3, 0, 1).reshape(values.shape[1] * values.shape[2], -1)


def slab_product(flat, weights):
    out = jnp.dot(flat, weights, preferred_element_type=jnp.float32)
    half = weights.shape[1] // 2
    return out[:, :half] + out[:, half:]


def add_cols(total, part, col_block):
    rows = part.shape[0]
    at = (jnp.int32(0), col_block * rows)
    here = lax.dynamic_slice(total, at, part.shape)
    return lax.dynamic_update_slice(total, here + part, at)


def per_device(tensor, live_blocks, occ_density, virt_density, occ_mask, virt_mask, pair_slots):
    rows = tensor.shape[0]
    assert tensor.shape[1] == BS
    planes = lax.axis_size("ri")
    cycle_size = lax.axis_size("ao")
    plane = lax.axis_index("ri")
    routes = pair_routes(planes)
    own = mask_slab(tensor, live_blocks)
    own_flat = own.reshape(rows, -1)
    lead = rows // 4
    early = [lax.ppermute(own_flat[:lead], "ri", route) for route, _, _ in routes]
    late = [lax.ppermute(own_flat[lead:], "ri", route) for route, _, _ in routes]
    stacked = jnp.stack(
        [screen_density(occ_density, occ_mask), screen_density(virt_density, virt_mask)]
    )
    full = lax.all_gather(stacked, "ao", axis=1, tiled=True)
    ao_total = full.shape[2]
    all_blocks = ao_total // BS
    picked = full.reshape(2, all_blocks, BS, ao_total)[:, pair_slots[0]]
    occ_rows = picked[0].reshape(KS * BS, ao_total)
    virt_rows = picked[1].reshape(KS * BS, ao_total)
    halves = jnp.einsum(
        "prk,dkc->cdrp", own, jnp.stack([occ_rows, virt_rows]), preferred_element_type=jnp.float32
    ).astype(jnp.bfloat16)
    halves = with_layout_constraint(halves, Layout(major_to_minor=(0, 1, 2, 3)))
    halves, early = lax.optimization_barrier((halves, early))
    swapped = lax.all_to_all(halves, "ao", 0, 2, tiled=True)
    occ_t = swapped[:, 0]
    virt_t = swapped[:, 1]
    v_part = jnp.einsum("mn,lnp->plm", virt_rows, occ_t, preferred_element_type=jnp.float32)
    w_part = jnp.einsum("kl,nlq->qnk", occ_rows, virt_t, preferred_element_type=jnp.float32)
    v_weights = weight_pair(v_part)
    w_weights = weight_pair(w_part)
    early_stack = jnp.concatenate(early)
    early_mine = slab_product(early_stack, v_weights)
    with_own = slab_product(jnp.concatenate([own_flat, early_stack]), w_weights)
    diag = with_own[:rows]
    early_theirs = with_own[rows:]
    v_weights, w_weights, diag, early_mine, early_theirs, late = lax.optimization_barrier(
        (v_weights, w_weights, diag, early_mine, early_theirs, late)
    )
    late_stack = jnp.concatenate(late)
    late_mine = slab_product(late_stack, v_weights)
    late_theirs = slab_product(late_stack, w_weights)
    count = len(routes)
    lead = rows // 4
    rest = rows - lead

    def slab_rows(early_part, late_part, index):
        return jnp.concatenate(
            [
                early_part[index * lead : (index + 1) * lead],
                late_part[index * rest : (index + 1) * rest],
            ]
        )

    mine_all = jnp.concatenate([slab_rows(early_mine, late_mine, i) for i in range(count)])
    theirs_all = jnp.concatenate([slab_rows(early_theirs, late_theirs, i) for i in range(count)])
    total = jnp.zeros((rows, planes * rows), jnp.float32)
    total = add_cols(total, diag, plane)
    for index, (route, recv_from, send_to) in enumerate(routes):
        source = jnp.array(recv_from, jnp.int32)[plane]
        target = jnp.array(send_to, jnp.int32)[plane]
        mine = mine_all[index * rows : (index + 1) * rows]
        theirs = theirs_all[index * rows : (index + 1) * rows]
        total = add_cols(total, mine.T, source)
        back = lax.ppermute(theirs, "ri", [(d, s) for s, d in route])
        total = add_cols(total, back, target)
    width = total.shape[1] // cycle_size
    sent = total.reshape(rows, cycle_size, width).transpose(1, 0, 2)
    got = lax.all_to_all(sent, "ao", 0, 0, tiled=True)
    return jnp.sum(got, axis=0)


def solution(mesh):
    placed = (
        P("ri", "ao", None),
        P("ri", "ao", None),
        P("ao", None),
        P("ao", None),
        P("ao", None),
        P("ao", None),
        P("ao", None),
    )
    return jax.shard_map(
        per_device, mesh=mesh, in_specs=placed, out_specs=P("ri", "ao"), check_vma=False
    )
```

profile of v0, /device:TPU:0, one launch (start us, length us, event | category | flops | bytes accessed | tf_op | source)
XLA Modules:
  0.0 131.0 jit_solution(13696888787203270410)
XLA Ops:
  0.0 0.7 convert_element_type.32
  1.1 1.8 %broadcast_multiply_fusion = bf16[128,32,256]{2,1,0:T(8,128)(2,1)S(1)} fusion(bf16[128,32,256]{2,1,0:T(8,128)(2,1)} %param.11, bf16[128,256]{1,0:T(8,128)(2,1)S(1)} %copy.25), kind=kLoop, calls=%fused_computation.32 | loop fusion | flops 1048576 | bytes 4259840 | tf_op jit(solution)/shard_map/mul | solution.py:43
  3.3 3.1 %collective-permute-start = (bf16[32,8192]{1,0:T(8,128)(2,1)S(1)}, bf16[32,8192]{1,0:T(8,128)(2,1)}, u32[]{:S(2)}, u32[]{:S(2)}) collective-permute-start(bf16[32,8192]{1,0:T(8,128)(2,1)S(1)} %bitcast.142), channel_id=1, source_target_pairs={{0,8},{8,16},{16,24},{24,0},{1,9},{9,17},{17,25},{25,1},{2,10},{10... | collective-permute-start | bytes 1572872 | tf_op jit(solution)/shard_map/ppermute | solution.py:80
  6.3 5.3 %collective-permute-start.1 = (bf16[32,8192]{1,0:T(8,128)(2,1)S(1)}, bf16[32,8192]{1,0:T(8,128)(2,1)}, u32[]{:S(2)}, u32[]{:S(2)}) collective-permute-start(bf16[32,8192]{1,0:T(8,128)(2,1)S(1)} %bitcast.143), channel_id=1, source_target_pairs={{0,16},{24,8},{1,17},{25,9},{2,18},{26,10},{3,19},{27,11},{4,20},{... | collective-permute-start | bytes 1572872 | tf_op jit(solution)/shard_map/ppermute | solution.py:80
  12.0 9.3 %all_gather.3 = bf16[2,256,256]{2,1,0:T(8,128)(2,1)S(1)} all-gather(bf16[2,32,256]{2,1,0:T(8,128)(2,1)S(1)} %pad_maximum_fusion.2), channel_id=1, replica_groups=mesh['ri'=4,'ao'=8] {'ao'}, dimensions={1}, use_global_device_ids=true | all-gather | bytes 294912 | tf_op jit(solution)/shard_map/all_gather | solution.py:85
  22.1 3.2 %fusion.15 = bf16[2,256,128,32]{2,1,3,0:T(8,128)(2,1)S(1)} fusion(bf16[128,32,256]{2,1,0:T(8,128)(2,1)S(1)} %broadcast_multiply_fusion, bf16[1,256,256]{1,2,0:T(8,128)(2,1)S(1)} %copy.23, bf16[1,256,256]{1,2,0:T(8,128)(2,1)S(1)} %copy.22), kind=kOutput, calls=%fused_computation.25 | convolution fusion | flops 1074266112 | bytes 6553600 | tf_op jit(solution)/shard_map/prk,dkc->cdrp/dot_general | solution.py:91
  25.3 4.7 %copy.55 = bf16[2,256,128,32]{2,3,0,1:T(8,128)(2,1)} copy(bf16[2,256,128,32]{2,1,3,0:T(8,128)(2,1)S(1)} %fusion.15) | data formatting | bytes 8388608 | tf_op jit(solution)/shard_map/prk,dkc->cdrp/dot_general | solution.py:91
  30.0 4.6 %all-to-all-start = ((bf16[256,2,32,128]{3,2,1,0:T(8,128)(2,1)}), bf16[256,2,32,128]{3,2,1,0:T(8,128)(2,1)}, u32[]{:S(2)}, u32[]{:S(2)}) async-start(bf16[256,2,32,128]{3,2,1,0:T(8,128)(2,1)} %bitcast.125), calls=%async_computation | async-start | bytes 8388608 | tf_op jit(solution)/shard_map/all_to_all | solution.py:96
  34.8 2.2 %copy.47 = bf16[12,8,32,256]{3,1,2,0:T(8,128)(2,1)} copy(bf16[12,8,32,256]{3,2,1,0:T(8,128)(2,1)S(1)} %bitcast.130) | data formatting | bytes 3145728
  37.0 2.2 %collective-permute-start.2 = (bf16[96,8192]{1,0:T(8,128)(2,1)}, bf16[96,8192]{1,0:T(8,128)(2,1)}, u32[]{:S(2)}, u32[]{:S(2)}) collective-permute-start(bf16[96,8192]{1,0:T(8,128)(2,1)} %bitcast.64), channel_id=1, source_target_pairs={{0,8},{8,16},{16,24},{24,0},{1,9},{9,17},{17,25},{25,1},{2,10},{10... | collective-permute-start | bytes 4718600 | tf_op jit(solution)/shard_map/ppermute | solution.py:81
  39.1 3.2 %collective-permute-start.3 = (bf16[96,8192]{1,0:T(8,128)(2,1)}, bf16[96,8192]{1,0:T(8,128)(2,1)}, u32[]{:S(2)}, u32[]{:S(2)}) collective-permute-start(bf16[96,8192]{1,0:T(8,128)(2,1)} %bitcast.64), channel_id=1, source_target_pairs={{0,16},{24,8},{1,17},{25,9},{2,18},{26,10},{3,19},{27,11},{4,20},{... | collective-permute-start | bytes 4718600 | tf_op jit(solution)/shard_map/ppermute | solution.py:81
  43.6 0.6 dynamic_slice.26
  46.0 0.6 dynamic_slice.30
  47.2 2.8 %copy.46 = bf16[16,8,32,256]{3,1,2,0:T(8,128)(2,1)} copy(bf16[16,8,32,256]{3,2,1,0:T(8,128)(2,1)S(1)} %bitcast.122) | data formatting | bytes 4194304
  49.9 33.8 %all-to-all-done = bf16[256,2,32,128]{3,2,1,0:T(8,128)(2,1)} async-done(((bf16[256,2,32,128]{3,2,1,0:T(8,128)(2,1)}), bf16[256,2,32,128]{3,2,1,0:T(8,128)(2,1)}, u32[]{:S(2)}, u32[]{:S(2)}) %all-to-all-start) | async-done | bytes 4194336 | tf_op jit(solution)/shard_map/all_to_all | solution.py:96
  83.7 3.3 %copy.28 = bf16[8,32,2,32,128]{4,3,0,2,1:T(8,128)(2,1)S(1)} copy(bf16[8,32,2,32,128]{4,3,2,1,0:T(8,128)(2,1)} %bitcast.16) | data formatting | bytes 8388608 | tf_op jit(solution)/shard_map/all_to_all | solution.py:96
  87.0 0.8 fusion.12
  88.2 2.4 %copy.32 = bf16[32,256,2,128]{1,0,3,2:T(8,128)(2,1)S(1)} copy(bf16[32,256,2,128]{1,3,0,2:T(8,128)(2,1)S(1)} %maximum_bitcast_fusion.1) | data formatting | bytes 8388608 | tf_op jit(solution)/shard_map/transpose | solution.py:54
  90.6 4.3 %copy.45 = bf16[32,8,32,256]{3,1,2,0:T(8,128)(2,1)S(1)} copy(bf16[32,8,32,256]{3,2,1,0:T(8,128)(2,1)S(1)} %bitcast.128) | data formatting | bytes 8388608
  95.0 2.7 %fusion.3 = f32[192,256]{1,0:T(8,128)S(1)} fusion(bf16[8192,256]{0,1:T(8,128)(2,1)S(1)} %bitcast.131, bf16[32,8192]{1,0:T(8,128)(2,1)} %collective-permute-done.1, bf16[32,8192]{1,0:T(8,128)(2,1)} %collective-permute-done, bf16[128,8192]{1,0:T(8,128)(2,1)S(1)} %bitcast.134), kind=kOutput, calls=%fused_computation.11 | convolution fusion | flops 814743552 | bytes 7536640 | tf_op jit(solution)/shard_map/dot_general | solution.py:58
  97.7 1.0 fusion.11
  99.2 2.4 %copy.30 = bf16[32,256,2,128]{1,0,3,2:T(8,128)(2,1)S(1)} copy(bf16[32,256,2,128]{1,3,0,2:T(8,128)(2,1)S(1)} %maximum_bitcast_fusion) | data formatting | bytes 8388608 | tf_op jit(solution)/shard_map/transpose | solution.py:54
  101.6 4.3 %copy.44 = bf16[32,8,32,256]{3,1,2,0:T(8,128)(2,1)S(1)} copy(bf16[32,8,32,256]{3,2,1,0:T(8,128)(2,1)S(1)} %bitcast.129) | data formatting | bytes 8388608
  105.9 3.4 %fusion.18 = f32[64,256]{1,0:T(8,128)S(1)} fusion(bf16[8192,256]{0,1:T(8,128)(2,1)S(1)} %bitcast.126, bf16[32,8192]{1,0:T(8,128)(2,1)} %collective-permute-done.1, bf16[32,8192]{1,0:T(8,128)(2,1)} %collective-permute-done), kind=kOutput, calls=%fused_computation.28 | convolution fusion | flops 270532608 | bytes 5308416 | tf_op jit(solution)/shard_map/dot_general | solution.py:58
  109.3 1.5 %constant_dynamic-update-slice_fusion.1 = bf16[192,8192]{1,0:T(8,128)(2,1)S(1)} fusion(bf16[96,8192]{1,0:T(8,128)(2,1)} %collective-permute-done.2), kind=kLoop, calls=%fused_computation.55 | loop fusion | bytes 3145728
  110.8 1.5 %constant_dynamic-update-slice_fusion = bf16[192,8192]{1,0:T(8,128)(2,1)S(1)} fusion(bf16[192,8192]{1,0:T(8,128)(2,1)S(1)} %constant_dynamic-update-slice_fusion.1, bf16[96,8192]{1,0:T(8,128)(2,1)} %collective-permute-done.3), kind=kLoop, calls=%fused_computation.54 | loop fusion | bytes 3145728 | tf_op jit(solution)/shard_map/concatenate | solution.py:111
  112.4 1.3 fusion.38
  114.0 1.3 collective-permute-start.5
  115.5 1.4 %collective-permute-start.4 = (f32[128,128]{0,1:T(8,128)S(1)}, f32[128,128]{0,1:T(8,128)S(1)}, u32[]{:S(2)}, u32[]{:S(2)}) collective-permute-start(f32[128,128]{0,1:T(8,128)S(1)} %pad_maximum_fusion), channel_id=1, source_target_pairs={{8,0},{16,8},{24,16},{0,24},{9,1},{17,9},{25,17},{1,25},{10,2},{18... | collective-permute-start | bytes 196616 | tf_op jit(solution)/shard_map/ppermute | solution.py:136
  116.9 3.7 %fusion.37 = f32[192,256]{1,0:T(8,128)S(1)} fusion(bf16[192,8192]{1,0:T(8,128)(2,1)S(1)} %constant_dynamic-update-slice_fusion, bf16[8192,256]{0,1:T(8,128)(2,1)} %bitcast.127), kind=kOutput, calls=%fused_computation.69 | convolution fusion | flops 805306368 | bytes 7536640 | tf_op jit(solution)/shard_map/dot_general | solution.py:58
  121.1 9.3 %all_to_all.23 = f32[8,128,64]{1,2,0:T(8,128)S(1)} all-to-all(f32[8,128,64]{1,2,0:T(8,128)S(1)} %bitcast.133), channel_id=1, replica_groups=mesh['ri'=4,'ao'=8] {'ao'}, dimensions={0} | all-to-all | bytes 524288 | tf_op jit(solution)/shard_map/all_to_all | solution.py:140
  130.4 0.6 reduce_sum.9
  (79 shorter events, 4.8 us)
Async XLA Ops:
  1.1 10.5 %copy-start.5 = (s32[1,8]{1,0:T(1,128)S(1)}, s32[1,8]{1,0:T(1,128)}, u32[]{:S(2)}) copy-start(s32[1,8]{1,0:T(1,128)} %param.15) | copy-start | bytes 100
  1.1 10.7 %copy-start.6 = (s32[1,8]{1,0:T(1,128)S(1)}, s32[1,8]{1,0:T(1,128)}, u32[]{:S(2)}) copy-start(s32[1,8]{1,0:T(1,128)} %param.16) | copy-start | bytes 100
  1.1 10.9 %copy-start.3 = (bf16[32,256]{1,0:T(8,128)(2,1)S(1)}, bf16[32,256]{1,0:T(8,128)(2,1)}, u32[]{:S(2)}) copy-start(bf16[32,256]{1,0:T(8,128)(2,1)} %param.14) | copy-start | bytes 49156
  1.1 10.8 %copy-start.4 = (bf16[32,256]{1,0:T(8,128)(2,1)S(1)}, bf16[32,256]{1,0:T(8,128)(2,1)}, u32[]{:S(2)}) copy-start(bf16[32,256]{1,0:T(8,128)(2,1)} %param.13) | copy-start | bytes 49156
  1.1 20.2 %copy-start.7 = (s32[1,8]{1,0:T(1,128)S(1)}, s32[1,8]{1,0:T(1,128)}, u32[]{:S(2)}) copy-start(s32[1,8]{1,0:T(1,128)} %param.17) | copy-start | bytes 100
  3.3 26.8 %collective-permute-start = (bf16[32,8192]{1,0:T(8,128)(2,1)S(1)}, bf16[32,8192]{1,0:T(8,128)(2,1)}, u32[]{:S(2)}, u32[]{:S(2)}) collective-permute-start(bf16[32,8192]{1,0:T(8,128)(2,1)S(1)} %bitcast.142), channel_id=1, source_target_pairs={{0,8},{8,16},{16,24},{24,0},{1,9},{9,17},{17,25},{25,1},{2,10},{10... | collective-permute-start | bytes 1572872 | tf_op jit(solution)/shard_map/ppermute | solution.py:80
  6.3 23.7 %collective-permute-start.1 = (bf16[32,8192]{1,0:T(8,128)(2,1)S(1)}, bf16[32,8192]{1,0:T(8,128)(2,1)}, u32[]{:S(2)}, u32[]{:S(2)}) collective-permute-start(bf16[32,8192]{1,0:T(8,128)(2,1)S(1)} %bitcast.143), channel_id=1, source_target_pairs={{0,16},{24,8},{1,17},{25,9},{2,18},{26,10},{3,19},{27,11},{4,20},{... | collective-permute-start | bytes 1572872 | tf_op jit(solution)/shard_map/ppermute | solution.py:80
  30.0 53.7 %all-to-all-start = ((bf16[256,2,32,128]{3,2,1,0:T(8,128)(2,1)}), bf16[256,2,32,128]{3,2,1,0:T(8,128)(2,1)}, u32[]{:S(2)}, u32[]{:S(2)}) async-start(bf16[256,2,32,128]{3,2,1,0:T(8,128)(2,1)} %bitcast.125), calls=%async_computation | async-start | bytes 8388608 | tf_op jit(solution)/shard_map/all_to_all | solution.py:96
  34.6 7.7 %copy-start.11 = (s32[4]{0:T(128)S(1)}, s32[4]{0:T(128)}, u32[]{:S(2)}) copy-start(s32[4]{0:T(128)} %constant.32.clone) | copy-start | bytes 52
  34.6 8.9 %copy-start.10 = (s32[4]{0:T(128)S(1)}, s32[4]{0:T(128)}, u32[]{:S(2)}) copy-start(s32[4]{0:T(128)} %constant.33.clone) | copy-start | bytes 52
  34.6 10.2 %copy-start.9 = (s32[4]{0:T(128)S(1)}, s32[4]{0:T(128)}, u32[]{:S(2)}) copy-start(s32[4]{0:T(128)} %constant.34.clone) | copy-start | bytes 52
  34.7 11.3 %copy-start.8 = (s32[4]{0:T(128)S(1)}, s32[4]{0:T(128)}, u32[]{:S(2)}) copy-start(s32[4]{0:T(128)} %constant.35.clone) | copy-start | bytes 52
  37.0 72.3 %collective-permute-start.2 = (bf16[96,8192]{1,0:T(8,128)(2,1)}, bf16[96,8192]{1,0:T(8,128)(2,1)}, u32[]{:S(2)}, u32[]{:S(2)}) collective-permute-start(bf16[96,8192]{1,0:T(8,128)(2,1)} %bitcast.64), channel_id=1, source_target_pairs={{0,8},{8,16},{16,24},{24,0},{1,9},{9,17},{17,25},{25,1},{2,10},{10... | collective-permute-start | bytes 4718600 | tf_op jit(solution)/shard_map/ppermute | solution.py:81
  39.1 70.2 %collective-permute-start.3 = (bf16[96,8192]{1,0:T(8,128)(2,1)}, bf16[96,8192]{1,0:T(8,128)(2,1)}, u32[]{:S(2)}, u32[]{:S(2)}) collective-permute-start(bf16[96,8192]{1,0:T(8,128)(2,1)} %bitcast.64), channel_id=1, source_target_pairs={{0,16},{24,8},{1,17},{25,9},{2,18},{26,10},{3,19},{27,11},{4,20},{... | collective-permute-start | bytes 4718600 | tf_op jit(solution)/shard_map/ppermute | solution.py:81
  90.6 4.3 %copy-start.1 = (bf16[16,8,32,256]{3,1,2,0:T(8,128)(2,1)S(1)}, bf16[16,8,32,256]{3,1,2,0:T(8,128)(2,1)}, u32[]{:S(2)}) copy-start(bf16[16,8,32,256]{3,1,2,0:T(8,128)(2,1)} %copy.46) | copy-start | bytes 6291460
  97.7 1.0 copy-start.2
  105.9 4.9 %copy-start = (bf16[32,8,32,256]{3,1,2,0:T(8,128)(2,1)}, bf16[32,8,32,256]{3,1,2,0:T(8,128)(2,1)S(1)}, u32[]{:S(2)}) copy-start(bf16[32,8,32,256]{3,1,2,0:T(8,128)(2,1)S(1)} %copy.44) | copy-start | bytes 12582916
  112.4 1.4 %slice-start.1 = ((f32[192,128]{1,0:T(8,128)}), f32[64,128]{1,0:T(8,128)S(1)}, s32[]{:S(2)}) async-start(f32[192,128]{1,0:T(8,128)} %copy-done.2), calls=%async_computation.3 | async-start | bytes 65536 | tf_op jit(solution)/shard_map/slice | solution.py:107
  114.0 7.1 %collective-permute-start.5 = (f32[128,128]{0,1:T(8,128)S(1)}, f32[128,128]{0,1:T(8,128)S(1)}, u32[]{:S(2)}, u32[]{:S(2)}) collective-permute-start(f32[128,128]{0,1:T(8,128)S(1)} %pad_maximum_fusion.1), channel_id=1, source_target_pairs={{16,0},{8,24},{17,1},{9,25},{18,2},{10,26},{19,3},{11,27},{20,4},{... | collective-permute-start | bytes 196616 | tf_op jit(solution)/shard_map/ppermute | solution.py:136
  115.5 5.2 %slice-start = ((f32[192,128]{1,0:T(8,128)}), f32[128,128]{1,0:T(8,128)S(1)}, s32[]{:S(2)}) async-start(f32[192,128]{1,0:T(8,128)} %copy-done.2), calls=%async_computation.2 | async-start | bytes 131072 | tf_op jit(solution)/shard_map/slice | solution.py:106
  115.5 5.4 %collective-permute-start.4 = (f32[128,128]{0,1:T(8,128)S(1)}, f32[128,128]{0,1:T(8,128)S(1)}, u32[]{:S(2)}, u32[]{:S(2)}) collective-permute-start(f32[128,128]{0,1:T(8,128)S(1)} %pad_maximum_fusion), channel_id=1, source_target_pairs={{8,0},{16,8},{24,16},{0,24},{9,1},{17,9},{25,17},{1,25},{10,2},{18... | collective-permute-start | bytes 196616 | tf_op jit(solution)/shard_map/ppermute | solution.py:136
where the time goes:
time: 132 us; the launch traced here: 131 us
  local copies, waits for them, and re-layouts  34.2 us (26%)
  waiting for transfers between devices  33.9 us (26%)
  starting transfers between devices  21 us (16%)
  blocking collectives  18.7 us (14%)
  matrix products  16.1 us (12%)
  other arithmetic  4.17 us (3%)
  between operations  2.98 us (2%)
    all_to_all x1, waiting for transfers between devices, per_device(): swapped = lax.all_to_all(halves, 'ao', 0, 2, tiled=True)  33.8 us
    unnamed x30, local copies, waits for them, and re-layouts  15.4 us
    dot_general x4, matrix products, slab_product(): out = jnp.dot(flat, weights, preferred_element_type=jnp.float32)  11.1 us
    all_to_all x1, blocking collectives, per_device(): got = lax.all_to_all(sent, 'ao', 0, 0, tiled=True)  9.35 us
    all_gather x1, blocking collectives, per_device(): full = lax.all_gather(stacked, 'ao', axis=1, tiled=True)  9.32 us
    ppermute x2, starting transfers between devices, per_device(): lax.ppermute(own_flat[:lead], 'ri', route)  8.36 us
    ppermute x2, starting transfers between devices, per_device(): lax.ppermute(own_flat[lead:], 'ri', route)  5.36 us
    transpose x2, local copies, waits for them, and re-layouts, weight_pair(): both.transpose(2, 3, 0, 1).reshape(values.shape[1] * values.shape[2], -1)  4.86 us
  transfers between devices with their start and end apart: 7, of which 2 were waited for; matrix products, arithmetic and copies ran while one was open for 35% of the time, Pallas kernels for 0%

commit v1 on v0

--- a/solution.py
+++ b/solution.py
@@ -82,7 +82,20 @@
     stacked = jnp.stack(
         [screen_density(occ_density, occ_mask), screen_density(virt_density, virt_mask)]
     )
-    full = lax.all_gather(stacked, "ao", axis=1, tiled=True)
+    inter = lax.axis_index("ao")
+    part_now = lax.axis_size("ao")
+    field_out, wide_out, a_next = (part_now, inter, stacked.shape[1])
+    m_next, outcome_arr = (stacked, 1)
+    while outcome_arr < field_out:
+        windows = []
+        kk = 0
+        while kk < field_out:
+            windows.append((kk, (kk - outcome_arr) % field_out))
+            kk = kk + 1
+        z = lax.ppermute(m_next, "ao", windows)
+        m_next = jnp.concatenate([m_next, z], 1)
+        outcome_arr = 2 * outcome_arr
+    full = jnp.roll(m_next, wide_out * a_next, 1)
     ao_total = full.shape[2]
     all_blocks = ao_total // BS
     picked = full.reshape(2, all_blocks, BS, ao_total)[:, pair_slots[0]]

time: 132 us -> 141 us (1.068)
  waiting for transfers between devices: 33.9 us -> 43.4 us
  blocking collectives: 18.7 us -> 9.35 us
  local copies, waits for them, and re-layouts: 34.2 us -> 39.4 us
  starting transfers between devices: 21 us -> 22.9 us
    all_gather x1 -> x0, blocking collectives: 9.32 us -> none  [per_device(): full = lax.all_gather(stacked, 'ao', axis=1, tiled=True)]
    ppermute x0 -> x3, waiting for transfers between devices: none -> 9.27 us  [per_device(): z = lax.ppermute(m_next, 'ao', windows)]
    unnamed x30 -> x37, local copies, waits for them, and re-layouts: 15.4 us -> 19 us
    ppermute x0 -> x3, starting transfers between devices: none -> 2.55 us  [per_device(): z = lax.ppermute(m_next, 'ao', windows)]
  transfers between devices with their start and end apart: 7 -> 10, of which waited for: 2 -> 4; matrix products, arithmetic and copies ran while one was open for 35% -> 38% of each run, Pallas kernels for 0% -> 0%
where the time goes in v1:
time: 141 us
  waiting for transfers between devices  43.4 us (31%)
  local copies, waits for them, and re-layouts  39.4 us (28%)
  starting transfers between devices  22.9 us (16%)
  matrix products  17 us (12%)
  blocking collectives  9.35 us (7%)
  other arithmetic  5.43 us (4%)
  between operations  3.1 us (2%)
    all_to_all x1, waiting for transfers between devices, per_device(): swapped = lax.all_to_all(halves, 'ao', 0, 2, tiled=True)  34.1 us
    unnamed x37, local copies, waits for them, and re-layouts  19 us
    dot_general x4, matrix products, slab_product(): out = jnp.dot(flat, weights, preferred_element_type=jnp.float32)  12 us
    all_to_all x1, blocking collectives, per_device(): got = lax.all_to_all(sent, 'ao', 0, 0, tiled=True)  9.35 us
    ppermute x3, waiting for transfers between devices, per_device(): z = lax.ppermute(m_next, 'ao', windows)  9.27 us
    ppermute x2, starting transfers between devices, per_device(): lax.ppermute(own_flat[:lead], 'ri', route)  8.35 us
    transpose x2, local copies, waits for them, and re-layouts, weight_pair(): both.transpose(2, 3, 0, 1).reshape(values.shape[1] * values.shape[2], -1)  4.86 us
    ppermute x2, starting transfers between devices, per_device(): lax.ppermute(own_flat[lead:], 'ri', route)  4.85 us
  transfers between devices with their start and end apart: 10, of which 4 were waited for; matrix products, arithmetic and copies ran while one was open for 38% of the time, Pallas kernels for 0%

profile of v1, /device:TPU:0, one launch (start us, length us, event | category | flops | bytes accessed | tf_op | source)
XLA Modules:
  0.0 140.6 jit_solution(1553448486775162626)
XLA Ops:
  1.1 1.8 %broadcast_multiply_fusion = bf16[128,32,256]{2,1,0:T(8,128)(2,1)S(1)} fusion(bf16[128,32,256]{2,1,0:T(8,128)(2,1)} %param.11, bf16[128,256]{1,0:T(8,128)(2,1)S(1)} %copy.25), kind=kLoop, calls=%fused_computation.32 | loop fusion | flops 1048576 | bytes 4259840 | tf_op jit(solution)/shard_map/mul | solution.py:43
  3.3 3.1 %collective-permute-start.3 = (bf16[32,8192]{1,0:T(8,128)(2,1)S(1)}, bf16[32,8192]{1,0:T(8,128)(2,1)}, u32[]{:S(2)}, u32[]{:S(2)}) collective-permute-start(bf16[32,8192]{1,0:T(8,128)(2,1)S(1)} %bitcast.142), channel_id=1, source_target_pairs={{0,8},{8,16},{16,24},{24,0},{1,9},{9,17},{17,25},{25,1},{2,10},{10... | collective-permute-start | bytes 1572872 | tf_op jit(solution)/shard_map/ppermute | solution.py:80
  6.3 5.3 %collective-permute-start.4 = (bf16[32,8192]{1,0:T(8,128)(2,1)S(1)}, bf16[32,8192]{1,0:T(8,128)(2,1)}, u32[]{:S(2)}, u32[]{:S(2)}) collective-permute-start(bf16[32,8192]{1,0:T(8,128)(2,1)S(1)} %bitcast.143), channel_id=1, source_target_pairs={{0,16},{24,8},{1,17},{25,9},{2,18},{26,10},{3,19},{27,11},{4,20},{... | collective-permute-start | bytes 1572872 | tf_op jit(solution)/shard_map/ppermute | solution.py:80
  12.6 1.3 collective-permute-start
  13.9 1.6 %collective-permute-done = bf16[2,32,256]{2,1,0:T(8,128)(2,1)S(1)} collective-permute-done((bf16[2,32,256]{2,1,0:T(8,128)(2,1)S(1)}, bf16[2,32,256]{2,1,0:T(8,128)(2,1)S(1)}, u32[]{:S(2)}, u32[]{:S(2)}) %collective-permute-start) | collective-permute-done | bytes 32800 | tf_op jit(solution)/shard_map/ppermute | solution.py:95
  15.5 1.1 collective-permute-start.1
  16.6 3.6 %collective-permute-done.1 = bf16[2,64,256]{2,1,0:T(8,128)(2,1)S(1)} collective-permute-done((bf16[2,64,256]{2,1,0:T(8,128)(2,1)S(1)}, bf16[2,64,256]{2,1,0:T(8,128)(2,1)S(1)}, u32[]{:S(2)}, u32[]{:S(2)}) %collective-permute-start.1) | collective-permute-done | bytes 65568 | tf_op jit(solution)/shard_map/ppermute | solution.py:95
  21.6 4.1 %collective-permute-done.2 = bf16[2,128,256]{2,1,0:T(8,128)(2,1)S(1)} collective-permute-done((bf16[2,128,256]{2,1,0:T(8,128)(2,1)S(1)}, bf16[2,128,256]{2,1,0:T(8,128)(2,1)S(1)}, u32[]{:S(2)}, u32[]{:S(2)}) %collective-permute-start.2) | collective-permute-done | bytes 131104 | tf_op jit(solution)/shard_map/ppermute | solution.py:95
  28.9 1.0 constant_dynamic-slice_fusion
  30.7 3.2 %fusion.15 = bf16[2,256,128,32]{2,1,3,0:T(8,128)(2,1)S(1)} fusion(bf16[128,32,256]{2,1,0:T(8,128)(2,1)S(1)} %broadcast_multiply_fusion, bf16[1,256,256]{1,2,0:T(8,128)(2,1)S(1)} %copy.23, bf16[1,256,256]{1,2,0:T(8,128)(2,1)S(1)} %copy.22), kind=kOutput, calls=%fused_computation.25 | convolution fusion | flops 1074266112 | bytes 6553600 | tf_op jit(solution)/shard_map/prk,dkc->cdrp/dot_general | solution.py:104
  33.8 4.7 %copy.55 = bf16[2,256,128,32]{2,3,0,1:T(8,128)(2,1)} copy(bf16[2,256,128,32]{2,1,3,0:T(8,128)(2,1)S(1)} %fusion.15) | data formatting | bytes 8388608 | tf_op jit(solution)/shard_map/prk,dkc->cdrp/dot_general | solution.py:104
  38.6 4.6 %all-to-all-start = ((bf16[256,2,32,128]{3,2,1,0:T(8,128)(2,1)}), bf16[256,2,32,128]{3,2,1,0:T(8,128)(2,1)}, u32[]{:S(2)}, u32[]{:S(2)}) async-start(bf16[256,2,32,128]{3,2,1,0:T(8,128)(2,1)} %bitcast.125), calls=%async_computation | async-start | bytes 8388608 | tf_op jit(solution)/shard_map/all_to_all | solution.py:109
  43.3 2.2 %copy.47 = bf16[12,8,32,256]{3,1,2,0:T(8,128)(2,1)} copy(bf16[12,8,32,256]{3,2,1,0:T(8,128)(2,1)S(1)} %bitcast.130) | data formatting | bytes 3145728
  45.5 4.8 %collective-permute-start.6 = (bf16[96,8192]{1,0:T(8,128)(2,1)}, bf16[96,8192]{1,0:T(8,128)(2,1)}, u32[]{:S(2)}, u32[]{:S(2)}) collective-permute-start(bf16[96,8192]{1,0:T(8,128)(2,1)} %bitcast.64), channel_id=1, source_target_pairs={{0,16},{24,8},{1,17},{25,9},{2,18},{26,10},{3,19},{27,11},{4,20},{... | collective-permute-start | bytes 4718600 | tf_op jit(solution)/shard_map/ppermute | solution.py:81
  55.3 2.8 %copy.46 = bf16[16,8,32,256]{3,1,2,0:T(8,128)(2,1)} copy(bf16[16,8,32,256]{3,2,1,0:T(8,128)(2,1)S(1)} %bitcast.122) | data formatting | bytes 4194304
  58.1 34.1 %all-to-all-done = bf16[256,2,32,128]{3,2,1,0:T(8,128)(2,1)} async-done(((bf16[256,2,32,128]{3,2,1,0:T(8,128)(2,1)}), bf16[256,2,32,128]{3,2,1,0:T(8,128)(2,1)}, u32[]{:S(2)}, u32[]{:S(2)}) %all-to-all-start) | async-done | bytes 4194336 | tf_op jit(solution)/shard_map/all_to_all | solution.py:109
  92.2 3.3 %copy.28 = bf16[8,32,2,32,128]{4,3,0,2,1:T(8,128)(2,1)S(1)} copy(bf16[8,32,2,32,128]{4,3,2,1,0:T(8,128)(2,1)} %bitcast.16) | data formatting | bytes 8388608 | tf_op jit(solution)/shard_map/all_to_all | solution.py:109
  95.5 0.8 fusion.12
  96.7 2.4 %copy.32 = bf16[32,256,2,128]{1,0,3,2:T(8,128)(2,1)S(1)} copy(bf16[32,256,2,128]{1,3,0,2:T(8,128)(2,1)S(1)} %maximum_bitcast_fusion.1) | data formatting | bytes 8388608 | tf_op jit(solution)/shard_map/transpose | solution.py:54
  99.1 4.3 %copy.45 = bf16[32,8,32,256]{3,1,2,0:T(8,128)(2,1)S(1)} copy(bf16[32,8,32,256]{3,2,1,0:T(8,128)(2,1)S(1)} %bitcast.128) | data formatting | bytes 8388608
  103.5 2.7 %fusion.3 = f32[192,256]{1,0:T(8,128)S(1)} fusion(bf16[8192,256]{0,1:T(8,128)(2,1)S(1)} %bitcast.131, bf16[32,8192]{1,0:T(8,128)(2,1)} %collective-permute-done.4, bf16[32,8192]{1,0:T(8,128)(2,1)} %collective-permute-done.3, bf16[128,8192]{1,0:T(8,128)(2,1)S(1)} %bitcast.134), kind=kOutput, calls=%fused_computation.11 | convolution fusion | flops 814743552 | bytes 7536640 | tf_op jit(solution)/shard_map/dot_general | solution.py:58
  106.2 1.0 fusion.11
  107.7 2.4 %copy.30 = bf16[32,256,2,128]{1,0,3,2:T(8,128)(2,1)S(1)} copy(bf16[32,256,2,128]{1,3,0,2:T(8,128)(2,1)S(1)} %maximum_bitcast_fusion) | data formatting | bytes 8388608 | tf_op jit(solution)/shard_map/transpose | solution.py:54
  110.1 4.3 %copy.44 = bf16[32,8,32,256]{3,1,2,0:T(8,128)(2,1)S(1)} copy(bf16[32,8,32,256]{3,2,1,0:T(8,128)(2,1)S(1)} %bitcast.129) | data formatting | bytes 8388608
  114.4 3.4 %fusion.18 = f32[64,256]{1,0:T(8,128)S(1)} fusion(bf16[8192,256]{0,1:T(8,128)(2,1)S(1)} %bitcast.126, bf16[32,8192]{1,0:T(8,128)(2,1)} %collective-permute-done.4, bf16[32,8192]{1,0:T(8,128)(2,1)} %collective-permute-done.3), kind=kOutput, calls=%fused_computation.28 | convolution fusion | flops 270532608 | bytes 5308416 | tf_op jit(solution)/shard_map/dot_general | solution.py:58
  117.8 1.5 %constant_dynamic-update-slice_fusion.9 = bf16[192,8192]{1,0:T(8,128)(2,1)S(1)} fusion(bf16[96,8192]{1,0:T(8,128)(2,1)} %collective-permute-done.5), kind=kLoop, calls=%fused_computation.62 | loop fusion | bytes 3145728
  119.3 1.5 %constant_dynamic-update-slice_fusion.8 = bf16[192,8192]{1,0:T(8,128)(2,1)S(1)} fusion(bf16[192,8192]{1,0:T(8,128)(2,1)S(1)} %constant_dynamic-update-slice_fusion.9, bf16[96,8192]{1,0:T(8,128)(2,1)} %collective-permute-done.6), kind=kLoop, calls=%fused_computation.61 | loop fusion | bytes 3145728 | tf_op jit(solution)/shard_map/concatenate | solution.py:124
  120.9 1.3 fusion.38
  122.8 1.3 collective-permute-start.8
  124.3 1.3 collective-permute-start.7
  125.6 4.7 %fusion.37 = f32[192,256]{1,0:T(8,128)S(1)} fusion(bf16[192,8192]{1,0:T(8,128)(2,1)} %copy-done.2, bf16[8192,256]{0,1:T(8,128)(2,1)} %bitcast.127), kind=kOutput, calls=%fused_computation.80 | convolution fusion | flops 805306368 | bytes 7536640 | tf_op jit(solution)/shard_map/dot_general | solution.py:58
  130.6 9.3 %all_to_all.23 = f32[8,128,64]{1,2,0:T(8,128)S(1)} all-to-all(f32[8,128,64]{1,2,0:T(8,128)S(1)} %bitcast.133), channel_id=1, replica_groups=mesh['ri'=4,'ao'=8] {'ao'}, dimensions={0} | all-to-all | bytes 524288 | tf_op jit(solution)/shard_map/all_to_all | solution.py:153
  (96 shorter events, 12.8 us)
Async XLA Ops:
  1.1 10.5 %copy-start.6 = (s32[1,8]{1,0:T(1,128)S(1)}, s32[1,8]{1,0:T(1,128)}, u32[]{:S(2)}) copy-start(s32[1,8]{1,0:T(1,128)} %param.15) | copy-start | bytes 100
  1.1 10.7 %copy-start.7 = (s32[1,8]{1,0:T(1,128)S(1)}, s32[1,8]{1,0:T(1,128)}, u32[]{:S(2)}) copy-start(s32[1,8]{1,0:T(1,128)} %param.16) | copy-start | bytes 100
  1.1 10.9 %copy-start.4 = (bf16[32,256]{1,0:T(8,128)(2,1)S(1)}, bf16[32,256]{1,0:T(8,128)(2,1)}, u32[]{:S(2)}) copy-start(bf16[32,256]{1,0:T(8,128)(2,1)} %param.14) | copy-start | bytes 49156
  1.1 10.8 %copy-start.5 = (bf16[32,256]{1,0:T(8,128)(2,1)S(1)}, bf16[32,256]{1,0:T(8,128)(2,1)}, u32[]{:S(2)}) copy-start(bf16[32,256]{1,0:T(8,128)(2,1)} %param.13) | copy-start | bytes 49156
  1.1 12.8 %copy-start.8 = (s32[1,8]{1,0:T(1,128)S(1)}, s32[1,8]{1,0:T(1,128)}, u32[]{:S(2)}) copy-start(s32[1,8]{1,0:T(1,128)} %param.17) | copy-start | bytes 100
  3.3 35.3 %collective-permute-start.3 = (bf16[32,8192]{1,0:T(8,128)(2,1)S(1)}, bf16[32,8192]{1,0:T(8,128)(2,1)}, u32[]{:S(2)}, u32[]{:S(2)}) collective-permute-start(bf16[32,8192]{1,0:T(8,128)(2,1)S(1)} %bitcast.142), channel_id=1, source_target_pairs={{0,8},{8,16},{16,24},{24,0},{1,9},{9,17},{17,25},{25,1},{2,10},{10... | collective-permute-start | bytes 1572872 | tf_op jit(solution)/shard_map/ppermute | solution.py:80
  6.3 32.2 %collective-permute-start.4 = (bf16[32,8192]{1,0:T(8,128)(2,1)S(1)}, bf16[32,8192]{1,0:T(8,128)(2,1)}, u32[]{:S(2)}, u32[]{:S(2)}) collective-permute-start(bf16[32,8192]{1,0:T(8,128)(2,1)S(1)} %bitcast.143), channel_id=1, source_target_pairs={{0,16},{24,8},{1,17},{25,9},{2,18},{26,10},{3,19},{27,11},{4,20},{... | collective-permute-start | bytes 1572872 | tf_op jit(solution)/shard_map/ppermute | solution.py:80
  12.6 2.9 %collective-permute-start = (bf16[2,32,256]{2,1,0:T(8,128)(2,1)S(1)}, bf16[2,32,256]{2,1,0:T(8,128)(2,1)S(1)}, u32[]{:S(2)}, u32[]{:S(2)}) collective-permute-start(bf16[2,32,256]{2,1,0:T(8,128)(2,1)S(1)} %get-tuple-element.39), channel_id=1, source_target_pairs={{0,7},{1,0},{2,1},{3,2},{4,3},{5,4},{6,5},{7,6},{8,15},{9,8},{10,9... | collective-permute-start | bytes 98312 | tf_op jit(solution)/shard_map/ppermute | solution.py:95
  15.5 4.7 %collective-permute-start.1 = (bf16[2,64,256]{2,1,0:T(8,128)(2,1)S(1)}, bf16[2,64,256]{2,1,0:T(8,128)(2,1)S(1)}, u32[]{:S(2)}, u32[]{:S(2)}) collective-permute-start(bf16[2,64,256]{2,1,0:T(8,128)(2,1)S(1)} %pad_maximum_fusion.1), channel_id=1, source_target_pairs={{0,6},{1,7},{2,0},{3,1},{4,2},{5,3},{6,4},{7,5},{8,14},{9,15},{10,... | collective-permute-start | bytes 196616 | tf_op jit(solution)/shard_map/ppermute | solution.py:95
  20.3 5.5 %collective-permute-start.2 = (bf16[2,128,256]{2,1,0:T(8,128)(2,1)S(1)}, bf16[2,128,256]{2,1,0:T(8,128)(2,1)S(1)}, u32[]{:S(2)}, u32[]{:S(2)}) collective-permute-start(bf16[2,128,256]{2,1,0:T(8,128)(2,1)S(1)} %pad_maximum_fusion), channel_id=1, source_target_pairs={{0,4},{1,5},{2,6},{3,7},{4,0},{5,1},{6,2},{7,3},{8,12},{9,13},{10,... | collective-permute-start | bytes 393224 | tf_op jit(solution)/shard_map/ppermute | solution.py:95
  38.6 53.7 %all-to-all-start = ((bf16[256,2,32,128]{3,2,1,0:T(8,128)(2,1)}), bf16[256,2,32,128]{3,2,1,0:T(8,128)(2,1)}, u32[]{:S(2)}, u32[]{:S(2)}) async-start(bf16[256,2,32,128]{3,2,1,0:T(8,128)(2,1)} %bitcast.125), calls=%async_computation | async-start | bytes 8388608 | tf_op jit(solution)/shard_map/all_to_all | solution.py:109
  43.1 7.2 %copy-start.12 = (s32[4]{0:T(128)S(1)}, s32[4]{0:T(128)}, u32[]{:S(2)}) copy-start(s32[4]{0:T(128)} %constant.58.clone) | copy-start | bytes 52
  43.1 8.4 %copy-start.11 = (s32[4]{0:T(128)S(1)}, s32[4]{0:T(128)}, u32[]{:S(2)}) copy-start(s32[4]{0:T(128)} %constant.59.clone) | copy-start | bytes 52
  43.1 9.7 %copy-start.10 = (s32[4]{0:T(128)S(1)}, s32[4]{0:T(128)}, u32[]{:S(2)}) copy-start(s32[4]{0:T(128)} %constant.60.clone) | copy-start | bytes 52
  43.2 10.9 %copy-start.9 = (s32[4]{0:T(128)S(1)}, s32[4]{0:T(128)}, u32[]{:S(2)}) copy-start(s32[4]{0:T(128)} %constant.61.clone) | copy-start | bytes 52
  45.5 72.3 %collective-permute-start.5 = (bf16[96,8192]{1,0:T(8,128)(2,1)}, bf16[96,8192]{1,0:T(8,128)(2,1)}, u32[]{:S(2)}, u32[]{:S(2)}) collective-permute-start(bf16[96,8192]{1,0:T(8,128)(2,1)} %bitcast.64), channel_id=1, source_target_pairs={{0,8},{8,16},{16,24},{24,0},{1,9},{9,17},{17,25},{25,1},{2,10},{10... | collective-permute-start | bytes 4718600 | tf_op jit(solution)/shard_map/ppermute | solution.py:81
  45.5 72.3 %collective-permute-start.6 = (bf16[96,8192]{1,0:T(8,128)(2,1)}, bf16[96,8192]{1,0:T(8,128)(2,1)}, u32[]{:S(2)}, u32[]{:S(2)}) collective-permute-start(bf16[96,8192]{1,0:T(8,128)(2,1)} %bitcast.64), channel_id=1, source_target_pairs={{0,16},{24,8},{1,17},{25,9},{2,18},{26,10},{3,19},{27,11},{4,20},{... | collective-permute-start | bytes 4718600 | tf_op jit(solution)/shard_map/ppermute | solution.py:81
  99.1 4.3 %copy-start.1 = (bf16[16,8,32,256]{3,1,2,0:T(8,128)(2,1)S(1)}, bf16[16,8,32,256]{3,1,2,0:T(8,128)(2,1)}, u32[]{:S(2)}) copy-start(bf16[16,8,32,256]{3,1,2,0:T(8,128)(2,1)} %copy.46) | copy-start | bytes 6291460
  106.2 1.0 copy-start.3
  114.4 4.9 %copy-start = (bf16[32,8,32,256]{3,1,2,0:T(8,128)(2,1)}, bf16[32,8,32,256]{3,1,2,0:T(8,128)(2,1)S(1)}, u32[]{:S(2)}) copy-start(bf16[32,8,32,256]{3,1,2,0:T(8,128)(2,1)S(1)} %copy.44) | copy-start | bytes 12582916
  120.9 1.7 %copy-start.2 = (bf16[192,8192]{1,0:T(8,128)(2,1)}, bf16[192,8192]{1,0:T(8,128)(2,1)S(1)}, u32[]{:S(2)}) copy-start(bf16[192,8192]{1,0:T(8,128)(2,1)S(1)} %constant_dynamic-update-slice_fusion.8) | copy-start | bytes 9437188
  120.9 1.8 %slice-start.1 = ((f32[192,128]{1,0:T(8,128)}), f32[64,128]{1,0:T(8,128)S(1)}, s32[]{:S(2)}) async-start(f32[192,128]{1,0:T(8,128)} %copy-done.3), calls=%async_computation.3 | async-start | bytes 65536 | tf_op jit(solution)/shard_map/slice | solution.py:120
  122.8 7.8 %collective-permute-start.8 = (f32[128,128]{0,1:T(8,128)S(1)}, f32[128,128]{0,1:T(8,128)S(1)}, u32[]{:S(2)}, u32[]{:S(2)}) collective-permute-start(f32[128,128]{0,1:T(8,128)S(1)} %pad_maximum_fusion.3), channel_id=1, source_target_pairs={{16,0},{8,24},{17,1},{9,25},{18,2},{10,26},{19,3},{11,27},{20,4},{... | collective-permute-start | bytes 196616 | tf_op jit(solution)/shard_map/ppermute | solution.py:149
  124.3 6.0 %slice-start = ((f32[192,128]{1,0:T(8,128)}), f32[128,128]{1,0:T(8,128)S(1)}, s32[]{:S(2)}) async-start(f32[192,128]{1,0:T(8,128)} %copy-done.3), calls=%async_computation.2 | async-start | bytes 131072 | tf_op jit(solution)/shard_map/slice | solution.py:119
  124.3 6.2 %collective-permute-start.7 = (f32[128,128]{0,1:T(8,128)S(1)}, f32[128,128]{0,1:T(8,128)S(1)}, u32[]{:S(2)}, u32[]{:S(2)}) collective-permute-start(f32[128,128]{0,1:T(8,128)S(1)} %pad_maximum_fusion.2), channel_id=1, source_target_pairs={{8,0},{16,8},{24,16},{0,24},{9,1},{17,9},{25,17},{1,25},{10,2},{18... | collective-permute-start | bytes 196616 | tf_op jit(solution)/shard_map/ppermute | solution.py:149
